TPU v7x, 512 devices: a whole 4x8x8 slice. The times are simulated.
512 devices in a mesh: member: 16 (over x_lo, y), dp: 32 (over z, x_hi, core).
Axes of the slice: x: 4 (x_hi: 2, x_lo: 2; x = x_hi * 2 + x_lo), y: 8, z: 8, core: 2. Of those that a mesh axis runs over, the one named last changes fastest.
Arguments:
- inputs: bfloat16 [8192, 64], P('dp'), may hold values from -6 to 6
- observed: float32 [64, 8192], P('member', 'dp'), may hold values from -6 to 6
- noise: bfloat16 [2, 32, 64, 8192], P(None, None, 'member', 'dp'), may hold values from -4 to 4
- w_in: float32 [32, 64, 4096], P('member', None, 'dp'), may hold values from -0.75 to 0.75
- b_in: float32 [32, 4096], P('member', 'dp'), may hold values from -3 to 3
- w_out: float32 [32, 64, 4096], P('member', None, 'dp'), may hold values from -0.09375 to 0.09375
- b_out: float32 [32, 64], P('member'), may hold values from -3 to 3
Outputs:
- new_w_in: float32 [32, 64, 4096], P('member', None, 'dp')
- new_b_in: float32 [32, 4096], P('member', 'dp')
- new_w_out: float32 [32, 64, 4096], P('member', None, 'dp')
- new_b_out: float32 [32, 64], P('member')
All inputs are finite; a program needn't handle non-finite values.
Results may differ from a plain program's by a relative error of at most 0.00056.
Values may be sent and summed in bfloat16 or wider, within the bound.
No kernel may reach another device: no remote copies, remote signals or barrier semaphores. Data moves between devices by JAX's collectives and lax.ppermute only.
A program may use at most 64 MiB of HBM per device.

v0:
```python
import jax
import jax.numpy as jnp
from jax import lax
from jax.sharding import PartitionSpec as P

UPDATES = 2
ridge_level = 0.5


def solve_gain(gram, cross):
    eye = jnp.eye(gram.shape[0], dtype=gram.dtype)
    factor = jnp.linalg.cholesky(gram + ridge_level * eye)
    middle = lax.linalg.triangular_solve(factor, cross, left_side=True, lower=True)
    return lax.linalg.triangular_solve(factor, middle, left_side=True, lower=True, transpose_a=True)


def pack(w_in, b_in, w_out, b_out):
    n = w_in.shape[0]
    return jnp.concatenate(
        [w_in.reshape(n, -1), w_out.reshape(n, -1), b_in.reshape(n, -1), b_out.reshape(n, -1)],
        axis=1,
    )


def unpack(flat, f_in, hid, outs):
    n = flat.shape[0]
    a = f_in * hid
    b = a + outs * hid
    c = b + hid
    return (
        flat[:, :a].reshape(n, f_in, hid),
        flat[:, b:c].reshape(n, hid),
        flat[:, a:b].reshape(n, outs, hid),
        flat[:, c:].reshape(n, outs),
    )


def predict(inputs, own_flat, b_out, f_in, hid, outs):
    n = own_flat.shape[0]
    a = f_in * hid
    b = a + outs * hid
    rounded = own_flat[:, : b + hid].astype(jnp.bfloat16)
    gathered = lax.all_gather(rounded, "dp", axis=0, tiled=False)
    d = gathered.shape[0]
    w_in = gathered[:, :, :a].reshape(d, n, f_in, hid)
    w_out = gathered[:, :, a:b].reshape(d, n, outs, hid)
    b_in = gathered[:, :, b : b + hid]
    pre = jnp.einsum("sf,dnfh->nsdh", inputs, w_in, preferred_element_type=jnp.float32)
    pre = pre + jnp.transpose(b_in, (1, 0, 2)).astype(jnp.float32)[:, None, :, :]
    hidden = jnp.tanh(pre).astype(jnp.bfloat16)
    pred = jnp.einsum("dnoh,nsdh->nos", w_out, hidden, preferred_element_type=jnp.float32)
    return pred + b_out[:, :, None]


def on_device(inputs, observed, noise, w_in, b_in, w_out, b_out):
    per_device = w_in.shape[0]
    f_in, hid = (w_in.shape[1], w_in.shape[2])
    outs = w_out.shape[1]
    count = observed.shape[0] * lax.axis_size("member") * observed.shape[1] * lax.axis_size("dp")
    first = lax.axis_index("member") * per_device
    own = pack(w_in, b_in, w_out, b_out)
    whole = lax.all_gather(own, "member", axis=0, tiled=True)
    for update in range(UPDATES):
        own_b_out = own[:, -outs:]
        predicted = predict(inputs, own, own_b_out, f_in, hid, outs)
        collected = lax.all_to_all(predicted, "member", split_axis=1, concat_axis=0, tiled=True)
        mean_pred = jnp.mean(collected, axis=0)
        anomaly = (collected - mean_pred[None]).reshape(collected.shape[0], -1)
        misfit = (observed[None] + noise[update].astype(jnp.float32) - collected).reshape(
            collected.shape[0], -1
        )
        gram_part = lax.dot_general(
            anomaly, anomaly, (((1,), (1,)), ((), ())), precision=lax.Precision.HIGHEST
        )
        cross_part = lax.dot_general(
            anomaly, misfit, (((1,), (1,)), ((), ())), precision=lax.Precision.HIGHEST
        )
        gram, cross = lax.psum((gram_part, cross_part), ("member", "dp"))
        gain = solve_gain(gram / count, cross / count)
        if update + 1 < UPDATES:
            moved = lax.dot_general(
                gain, whole, (((0,), (0,)), ((), ())), precision=lax.Precision.HIGHEST
            )
            whole = whole + moved
            own = lax.dynamic_slice_in_dim(whole, first, per_device, 0)
        else:
            columns = lax.dynamic_slice_in_dim(gain, first, per_device, 1)
            moved = lax.dot_general(
                columns, whole, (((0,), (0,)), ((), ())), precision=lax.Precision.HIGHEST
            )
            own = own + moved
    return unpack(own, f_in, hid, outs)


def solution(mesh):
    placed = (
        P("dp", None),
        P("member", "dp"),
        P(None, None, "member", "dp"),
        P("member", None, "dp"),
        P("member", "dp"),
        P("member", None, "dp"),
        P("member", None),
    )
    return jax.shard_map(
        on_device,
        mesh=mesh,
        in_specs=placed,
        out_specs=(
            P("member", None, "dp"),
            P("member", "dp"),
            P("member", None, "dp"),
            P("member", None),
        ),
        check_vma=False,
    )
```

profile of v0, /device:TPU:1, one launch (start us, length us, event | category | flops | bytes accessed | tf_op | source)
XLA Modules:
  0.0 511.3 jit_solution(14198276268625181387)
XLA Ops:
  7.9 0.8 convert.20
  8.8 0.8 convert.19
  10.4 1.0 copy_bitcast_fusion.2
  11.4 1.4 maximum_bitcast_fusion
  12.8 90.6 %all-gather.7.cloned.1.call-done = bf16[32,2,16512]{2,1,0:T(2,128)(2,1)} async-done(((bf16[1,2,16512]{2,1,0:T(2,128)(2,1)}), bf16[32,2,16512]{2,1,0:T(2,128)(2,1)}) %all-gather.7.cloned.1.call-update) | async-done | bytes 2113552 | tf_op jit(solution)/shard_map/all_gather | solution.py:43
  104.1 2.9 fusion.60
  108.8 2.5 fusion.20
  112.1 6.6 %all-to-all-start = ((f32[2,64,256]{2,0,1:T(2,128)}), f32[2,64,256]{2,0,1:T(2,128)S(1)}, u32[]{:S(2)}, u32[]{:S(2)}) async-start(f32[2,64,256]{2,0,1:T(2,128)} %copy.43), calls=%async_computation | async-start | bytes 262144 | tf_op jit(solution)/shard_map/all_to_all | solution.py:66
  118.8 47.6 %all-gather.9.cloned.1.call-done = f32[16,2,16576]{2,1,0:T(2,128)} async-done(((f32[1,2,16576]{2,1,0:T(2,128)}), f32[16,2,16576]{2,1,0:T(2,128)}) %all-gather.9.cloned.1.call-update) | async-done | bytes 2121744 | tf_op jit(solution)/shard_map/all_gather | solution.py:62
  166.4 3.7 reshape.128
  170.7 107.1 %all-reduce.1 = (f32[32,32]{0,1:T(8,128)S(1)}, f32[32,32]{0,1:T(8,128)S(1)}) all-reduce(f32[32,32]{0,1:T(8,128)S(1)} %convolution_bitcast_fusion.3, f32[32,32]{0,1:T(8,128)S(1)} %convolution_bitcast_fusion.2), channel_id=1, replica_groups=mesh['member'=16,'dp'=32] {'member','dp'}, use_global_device_ids=true, to_apply=%region_1.0 | all-reduce | flops 2048 | bytes 16384 | tf_op jit(solution)/shard_map/psum | solution.py:78
  277.9 2.9 cholesky.44
  282.1 2.4 custom-call.11
  285.0 4.2 convolution_add_fusion
  289.9 80.4 %all-gather.11.cloned.1.call-done = bf16[32,2,16512]{2,1,0:T(2,128)(2,1)} async-done(((bf16[1,2,16512]{2,1,0:T(2,128)(2,1)}), bf16[32,2,16512]{2,1,0:T(2,128)(2,1)}) %all-gather.11.cloned.1.call-update) | async-done | bytes 2113552 | tf_op jit(solution)/shard_map/all_gather | solution.py:43
  370.3 4.0 fusion.59
  374.4 2.6 reshape.116
  377.8 1.6 reshape.149
  379.4 3.2 fusion.1
  383.6 13.8 %all_to_all.30 = f32[2,64,256]{2,0,1:T(2,128)S(1)} all-to-all(f32[2,64,256]{2,0,1:T(2,128)S(1)} %copy.55), channel_id=1, replica_groups=mesh['member'=16,'dp'=32] {'member'}, dimensions={1} | all-to-all | bytes 262144 | tf_op jit(solution)/shard_map/all_to_all | solution.py:66
  398.0 96.0 %all-reduce = (f32[32,32]{0,1:T(8,128)S(1)}, f32[32,32]{0,1:T(8,128)S(1)}) all-reduce(f32[32,32]{0,1:T(8,128)S(1)} %convolution_bitcast_fusion.1, f32[32,32]{0,1:T(8,128)S(1)} %convolution_bitcast_fusion), channel_id=1, replica_groups=mesh['member'=16,'dp'=32] {'member','dp'}, use_global_device_ids=true, to_apply=%region_6.10 | all-reduce | flops 2048 | bytes 16384 | tf_op jit(solution)/shard_map/psum | solution.py:78
  494.1 2.9 cholesky.55
  498.4 2.4 custom-call.13
  501.3 1.1 convolution_add_fusion.1
  (64 shorter events, 14.5 us)
Async XLA Ops:
  7.2 101.6 %copy-start = (bf16[256,64]{0,1:T(8,128)(2,1)S(1)}, bf16[256,64]{0,1:T(8,128)(2,1)}, u32[]{:S(2)}) copy-start(bf16[256,64]{0,1:T(8,128)(2,1)} %param.12) | copy-start | bytes 98308
  7.2 96.2 %all-gather.7.cloned.1.call-start = ((), (), s32[]{:S(2)}) async-start(), calls=%async_computation.2 | async-start | bytes 2179584 | tf_op jit(solution)/shard_map/all_gather | solution.py:43
  10.3 156.0 %all-gather.9.cloned.1.call-start = ((), (), s32[]{:S(2)}) async-start(), calls=%async_computation.3 | async-start | bytes 2263040 | tf_op jit(solution)/shard_map/all_gather | solution.py:62
  107.1 1.7 copy-start.4
  108.8 9.9 %copy-start.2 = (bf16[2,32,4,256]{3,2,1,0:T(4,128)(2,1)S(1)}, bf16[2,32,4,256]{3,2,1,0:T(4,128)(2,1)}, u32[]{:S(2)}) copy-start(bf16[2,32,4,256]{3,2,1,0:T(4,128)(2,1)} %param.14) | copy-start | bytes 393220
  112.1 58.0 %all-to-all-start = ((f32[2,64,256]{2,0,1:T(2,128)}), f32[2,64,256]{2,0,1:T(2,128)S(1)}, u32[]{:S(2)}, u32[]{:S(2)}) async-start(f32[2,64,256]{2,0,1:T(2,128)} %copy.43), calls=%async_computation | async-start | bytes 262144 | tf_op jit(solution)/shard_map/all_to_all | solution.py:66
  118.6 251.7 %all-gather.11.cloned.1.call-start = ((), (), s32[]{:S(2)}) async-start(), calls=%async_computation.4 | async-start | bytes 2179584 | tf_op jit(solution)/shard_map/all_gather | solution.py:43
  118.7 51.4 %copy-start.3 = (f32[4,256]{1,0:T(4,128)S(1)}, f32[4,256]{1,0:T(4,128)}, u32[]{:S(2)}) copy-start(f32[4,256]{1,0:T(4,128)} %param.13) | copy-start | bytes 12292
  379.4 3.2 copy-start.1
Sparse Core Ops, SparseCore 0:
  11.4 91.9 all-gather.6
  105.5 60.8 all-gather.8
  290.0 80.3 all-gather.10
where the time goes:
time: 512 us; the launch traced here: 511 us
  waiting for transfers between devices  219 us (43%)
  blocking collectives  217 us (42%)
  local copies, waits for them, and re-layouts  21.8 us (4%)
  other arithmetic  19.5 us (4%)
  between operations  14 us (3%)
  matrix products  13.7 us (3%)
  starting transfers between devices  6.69 us (1%)
    psum x2, blocking collectives, on_device(): gram, cross = lax.psum((gram_part, cross_part), ('member', 'dp'))  203 us
    all_gather x2, waiting for transfers between devices, predict(): gathered = lax.all_gather(rounded, 'dp', axis=0, tiled=False)  171 us
    all_gather x1, waiting for transfers between devices, on_device(): whole = lax.all_gather(own, 'member', axis=0, tiled=True)  47.6 us
    all_to_all x1, blocking collectives, on_device(): lax.all_to_all(predicted, 'member', split_axis=1, concat_axis=0, tiled=True)  13.8 us
  transfers between devices with their start and end apart: 4, of which 3 were waited for; matrix products, arithmetic and copies ran while one was open for 3% of the time, Pallas kernels for 0%

commit v1 on v0

--- a/solution.py
+++ b/solution.py
@@ -59,7 +59,9 @@
     count = observed.shape[0] * lax.axis_size("member") * observed.shape[1] * lax.axis_size("dp")
     first = lax.axis_index("member") * per_device
     own = pack(w_in, b_in, w_out, b_out)
-    whole = lax.all_gather(own, "member", axis=0, tiled=True)
+    whole = jnp.concatenate(
+        lax.all_to_all(jnp.stack([own] * lax.axis_size("member")), "member", 0, 0), axis=0
+    )
     for update in range(UPDATES):
         own_b_out = own[:, -outs:]
         predicted = predict(inputs, own, own_b_out, f_in, hid, outs)

time: 512 us -> 466 us (0.910)
  waiting for transfers between devices: 219 us -> 170 us
  blocking collectives: 217 us -> 206 us
  starting transfers between devices: 6.69 us -> 14.2 us
    all_gather x1 -> x0, waiting for transfers between devices: 47.6 us -> none  [on_device(): whole = lax.all_gather(own, 'member', axis=0, tiled=True)]
    psum x2, blocking collectives: 203 us -> 192 us  [on_device(): gram, cross = lax.psum((gram_part, cross_part), ('member', 'dp'))]
    all_to_all x0 -> x1, starting transfers between devices: none -> 8.68 us  [on_device(): lax.all_to_all(jnp.stack([own] * lax.axis_size('member')), 'member', 0, 0)]
    all_gather x2, waiting for transfers between devices: 171 us -> 165 us  [predict(): gathered = lax.all_gather(rounded, 'dp', axis=0, tiled=False)]
  transfers between devices with their start and end apart: 4 -> 4, of which waited for: 3 -> 3; matrix products, arithmetic and copies ran while one was open for 3% -> 4% of each run, Pallas kernels for 0% -> 0%
where the time goes in v1:
time: 466 us; the launch traced here: 465 us
  blocking collectives  206 us (44%)
  waiting for transfers between devices  170 us (36%)
  local copies, waits for them, and re-layouts  26.3 us (6%)
  other arithmetic  18.9 us (4%)
  matrix products  15.3 us (3%)
  between operations  14.3 us (3%)
  starting transfers between devices  14.2 us (3%)
    psum x2, blocking collectives, on_device(): gram, cross = lax.psum((gram_part, cross_part), ('member', 'dp'))  192 us
    all_gather x2, waiting for transfers between devices, predict(): gathered = lax.all_gather(rounded, 'dp', axis=0, tiled=False)  165 us
    all_to_all x1, blocking collectives, on_device(): lax.all_to_all(predicted, 'member', split_axis=1, concat_axis=0, tiled=True)  13.8 us
  transfers between devices with their start and end apart: 4, of which 3 were waited for; matrix products, arithmetic and copies ran while one was open for 4% of the time, Pallas kernels for 0%

profile of v1, /device:TPU:1, one launch (start us, length us, event | category | flops | bytes accessed | tf_op | source)
XLA Modules:
  0.0 465.0 jit_solution(12937209590407473196)
XLA Ops:
  12.1 1.9 stack.2
  14.0 8.7 %all-to-all-start = ((f32[16,2,16576]{2,1,0:T(2,128)}), f32[16,2,16576]{2,1,0:T(2,128)S(1)}, u32[]{:S(2)}, u32[]{:S(2)}) async-start(f32[16,2,16576]{2,1,0:T(2,128)} %stack.2), calls=%async_computation | async-start | bytes 4259840 | tf_op jit(solution)/shard_map/all_to_all | solution.py:63
  22.7 84.6 %all-gather.5.cloned.1.call-done = bf16[32,2,16512]{2,1,0:T(2,128)(2,1)} async-done(((bf16[1,2,16512]{2,1,0:T(2,128)(2,1)}), bf16[32,2,16512]{2,1,0:T(2,128)(2,1)}) %all-gather.5.cloned.1.call-update) | async-done | bytes 2113552 | tf_op jit(solution)/shard_map/all_gather | solution.py:43
  108.0 4.1 fusion.60
  112.1 2.6 reshape.152
  114.7 1.6 reshape.151
  116.3 4.1 fusion.20
  121.2 5.4 %all-to-all-start.1 = ((f32[2,64,256]{2,0,1:T(2,128)}), f32[2,64,256]{2,0,1:T(2,128)S(1)}, u32[]{:S(2)}, u32[]{:S(2)}) async-start(f32[2,64,256]{2,0,1:T(2,128)} %copy.43), calls=%async_computation.1 | async-start | bytes 262144 | tf_op jit(solution)/shard_map/all_to_all | solution.py:68
  126.7 2.5 reshape.119
  129.2 4.8 %all-to-all-done.1 = f32[2,64,256]{2,0,1:T(2,128)S(1)} async-done(((f32[2,64,256]{2,0,1:T(2,128)}), f32[2,64,256]{2,0,1:T(2,128)S(1)}, u32[]{:S(2)}, u32[]{:S(2)}) %all-to-all-start.1) | async-done | bytes 131104 | tf_op jit(solution)/shard_map/all_to_all | solution.py:68
  134.7 96.2 %all-reduce.1 = (f32[32,32]{0,1:T(8,128)S(1)}, f32[32,32]{0,1:T(8,128)S(1)}) all-reduce(f32[32,32]{0,1:T(8,128)S(1)} %convolution_bitcast_fusion.3, f32[32,32]{0,1:T(8,128)S(1)} %convolution_bitcast_fusion.2), channel_id=1, replica_groups=mesh['member'=16,'dp'=32] {'member','dp'}, use_global_device_ids=true, to_apply=%region_1.0 | all-reduce | flops 2048 | bytes 16384 | tf_op jit(solution)/shard_map/psum | solution.py:80
  231.0 2.9 cholesky.44
  235.2 2.4 custom-call.11
  238.0 4.2 convolution_add_fusion
  243.0 80.7 %all-gather.7.cloned.1.call-done = bf16[32,2,16512]{2,1,0:T(2,128)(2,1)} async-done(((bf16[1,2,16512]{2,1,0:T(2,128)(2,1)}), bf16[32,2,16512]{2,1,0:T(2,128)(2,1)}) %all-gather.7.cloned.1.call-update) | async-done | bytes 2113552 | tf_op jit(solution)/shard_map/all_gather | solution.py:43
  323.7 4.0 fusion.59
  327.7 2.6 reshape.122
  331.1 1.6 reshape.153
  332.8 3.2 fusion.1
  337.0 13.8 %all_to_all.35 = f32[2,64,256]{2,0,1:T(2,128)S(1)} all-to-all(f32[2,64,256]{2,0,1:T(2,128)S(1)} %copy.55), channel_id=1, replica_groups=mesh['member'=16,'dp'=32] {'member'}, dimensions={1} | all-to-all | bytes 262144 | tf_op jit(solution)/shard_map/all_to_all | solution.py:68
  351.4 96.0 %all-reduce = (f32[32,32]{0,1:T(8,128)S(1)}, f32[32,32]{0,1:T(8,128)S(1)}) all-reduce(f32[32,32]{0,1:T(8,128)S(1)} %convolution_bitcast_fusion.1, f32[32,32]{0,1:T(8,128)S(1)} %convolution_bitcast_fusion), channel_id=1, replica_groups=mesh['member'=16,'dp'=32] {'member','dp'}, use_global_device_ids=true, to_apply=%region_6.10 | all-reduce | flops 2048 | bytes 16384 | tf_op jit(solution)/shard_map/psum | solution.py:80
  447.5 2.9 cholesky.55
  451.7 2.4 custom-call.13
  454.6 1.1 convolution_add_fusion.1
  (64 shorter events, 16.3 us)
Async XLA Ops:
  7.2 109.1 %copy-start = (bf16[256,64]{0,1:T(8,128)(2,1)S(1)}, bf16[256,64]{0,1:T(8,128)(2,1)}, u32[]{:S(2)}) copy-start(bf16[256,64]{0,1:T(8,128)(2,1)} %param.12) | copy-start | bytes 98308
  7.2 100.1 %all-gather.5.cloned.1.call-start = ((), (), s32[]{:S(2)}) async-start(), calls=%async_computation.3 | async-start | bytes 2179584 | tf_op jit(solution)/shard_map/all_gather | solution.py:43
  14.0 107.2 %all-to-all-start = ((f32[16,2,16576]{2,1,0:T(2,128)}), f32[16,2,16576]{2,1,0:T(2,128)S(1)}, u32[]{:S(2)}, u32[]{:S(2)}) async-start(f32[16,2,16576]{2,1,0:T(2,128)} %stack.2), calls=%async_computation | async-start | bytes 4259840 | tf_op jit(solution)/shard_map/all_to_all | solution.py:63
  112.0 4.2 copy-start.4
  116.3 10.3 %copy-start.2 = (bf16[2,32,4,256]{3,2,1,0:T(4,128)(2,1)S(1)}, bf16[2,32,4,256]{3,2,1,0:T(4,128)(2,1)}, u32[]{:S(2)}) copy-start(bf16[2,32,4,256]{3,2,1,0:T(4,128)(2,1)} %param.14) | copy-start | bytes 393220
  121.2 12.8 %all-to-all-start.1 = ((f32[2,64,256]{2,0,1:T(2,128)}), f32[2,64,256]{2,0,1:T(2,128)S(1)}, u32[]{:S(2)}, u32[]{:S(2)}) async-start(f32[2,64,256]{2,0,1:T(2,128)} %copy.43), calls=%async_computation.1 | async-start | bytes 262144 | tf_op jit(solution)/shard_map/all_to_all | solution.py:68
  126.6 197.1 %all-gather.7.cloned.1.call-start = ((), (), s32[]{:S(2)}) async-start(), calls=%async_computation.4 | async-start | bytes 2179584 | tf_op jit(solution)/shard_map/all_gather | solution.py:43
  126.7 7.4 %copy-start.3 = (f32[4,256]{1,0:T(4,128)S(1)}, f32[4,256]{1,0:T(4,128)}, u32[]{:S(2)}) copy-start(f32[4,256]{1,0:T(4,128)} %param.13) | copy-start | bytes 12292
  332.8 3.2 copy-start.1
Sparse Core Ops, SparseCore 0:
  11.4 95.8 all-gather.4
  243.0 80.6 all-gather.6
